TPU v7x, 32 devices: a whole 2x2x4 slice. The times are simulated.
32 devices in a mesh: panel: 2 (over y), lat: 4 (over z), lon: 4 (over x, core).
Axes of the slice: x: 2, y: 2, z: 4, core: 2. Of those that a mesh axis runs over, the one named last changes fastest.
Arguments:
- state: float32 [2, 7, 2, 256, 512], P('panel', None, None, 'lat', 'lon'), may hold values from -4 to 4
- source_slot: int32 [2, 4, 4, 768], P('panel', 'lat', 'lon'), may hold values from 0 to 3071, as said below
- donor_cell: int32 [2, 4, 4, 192], P('panel', 'lat', 'lon'), may hold values from 0 to 8000
- donor_frac: float32 [2, 4, 4, 2, 192], P('panel', 'lat', 'lon'), may hold values from 0 to 1
- donor_turn: float32 [2, 4, 4, 192], P('panel', 'lat', 'lon'), may hold values from -3.140625 to 3.140625
Outputs:
- new_state: float32 [2, 7, 2, 256, 512], P('panel', None, None, 'lat', 'lon')
Inputs may be any that keep to these rules, and one draw needn't show every extreme that they name: `source_slot`: entries name a partner panel donation (a * 4 + b) * 192 + s. For a device on an edge of its panel, the rim entries that lie on that edge name the donations that fill them; over a panel's whole border every donation of the partner panel is named exactly once. Other entries are unused.
All inputs are finite; a program needn't handle non-finite values.
Results may differ from a plain program's by a relative error of at most 0.00002.
Values sent between devices are 32-bit elements; how exact they have to be, the bound alone decides.
No kernel may reach another device: no remote copies, remote signals or barrier semaphores. Data moves between devices by JAX's collectives and lax.ppermute only.
A program may use at most 64 MiB of HBM per device.

v0:
```python
import jax
import jax.numpy as jnp
from jax import lax
from jax.sharding import PartitionSpec as P

viscosity = 0.05
resistivity = 0.05
diffusivity = 0.05
buoyancy = 0.5
time_step = 0.25
HIGHEST = lax.Precision.HIGHEST


def partner_2(block, axis, apart):
    count = lax.axis_size(axis)
    route = []
    for low in range(count):
        high = low | 1 << apart
        if high != low and high < count:
            route += [(low, high), (high, low)]
    return lax.ppermute(block, axis, route)


def shift(value, axis, step):
    size = lax.axis_size(axis)
    if step > 0:
        route = [(i, i + 1) for i in range(size - 1)]
    else:
        route = [(i + 1, i) for i in range(size - 1)]
    return lax.ppermute(value, axis, route)


def rate(up, mid, down, left, right):
    vert = jnp.concatenate([up, mid, down], axis=2)
    horz = jnp.concatenate([left, mid, right], axis=3)
    height = mid.shape[2]
    width = mid.shape[3]

    def lat_at(k):
        return vert[:, :, 2 + k : 2 + k + height, :]

    def lon_at(k):
        return horz[:, :, :, 2 + k : 2 + k + width]

    middle = mid
    d_lat = (8.0 * (lat_at(1) - lat_at(-1)) - (lat_at(2) - lat_at(-2))) / 12.0
    d_lon = (8.0 * (lon_at(1) - lon_at(-1)) - (lon_at(2) - lon_at(-2))) / 12.0
    padded = jnp.pad(middle, ((0, 0), (1, 1), (0, 0), (0, 0)))
    lap = lat_at(1) + lat_at(-1) + lon_at(1) + lon_at(-1) - 4.0 * middle
    lap = lap + padded[:, 2:] + padded[:, :-2] - 2.0 * middle
    adv_u = middle[1:2] * d_lat + middle[2:3] * d_lon
    adv_b = middle[4:5] * d_lat + middle[5:6] * d_lon
    moment = -adv_u[0:3] + adv_b[3:6] + viscosity * lap[0:3]
    induct = adv_b[0:3] - adv_u[3:6] + resistivity * lap[3:6]
    heat = -adv_u[6:7] + diffusivity * lap[6:7]
    first = moment[0:1] + buoyancy * middle[6:7]
    return jnp.concatenate([first, moment[1:3], induct, heat], axis=0)


def rotate(values, turn):
    cosine = jnp.cos(turn)
    sine = jnp.sin(turn)
    parts = [
        values[0],
        cosine * values[1] - sine * values[2],
        sine * values[1] + cosine * values[2],
        values[3],
        cosine * values[4] - sine * values[5],
        sine * values[4] + cosine * values[5],
        values[6],
    ]
    return jnp.stack(parts)


def per_device(state, source_slot, donor_cell, donor_frac, donor_turn):
    comps = state.shape[1]
    levels = state.shape[2]
    rows = state.shape[3]
    cols = state.shape[4]
    cells = donor_cell[0, 0, 0]
    frac_t = donor_frac[0, 0, 0, 0]
    frac_p = donor_frac[0, 0, 0, 1]
    turn = donor_turn[0, 0, 0]
    slots = source_slot[0, 0, 0]
    lat_pos = lax.axis_index("lat")
    lon_pos = lax.axis_index("lon")
    lat_count = lax.axis_size("lat")
    lon_count = lax.axis_size("lon")
    on_top = lat_pos == 0
    on_bottom = lat_pos == lat_count - 1
    on_left = lon_pos == 0
    on_right = lon_pos == lon_count - 1
    row = cells // (cols - 1)
    col = cells % (cols - 1)
    col_ids = jnp.arange(cols, dtype=jnp.int32)[None, :]
    row_ids = jnp.arange(rows, dtype=jnp.int32)[None, :]
    weight_lon = jnp.where(col_ids == col[:, None], (1.0 - frac_p)[:, None], 0.0) + jnp.where(
        col_ids == col[:, None] + 1, frac_p[:, None], 0.0
    )
    weight_lat = jnp.where(row_ids == row[:, None], (1.0 - frac_t)[:, None], 0.0) + jnp.where(
        row_ids == row[:, None] + 1, frac_t[:, None], 0.0
    )
    band = 2 * cols
    side = 2 * rows
    lat_slots = jnp.where(on_top, slots[0:band], slots[band : 2 * band])
    lon_slots = jnp.where(on_left, slots[2 * band : 2 * band + side], slots[2 * band + side :])
    wanted = jnp.concatenate([lat_slots, lon_slots])
    total = lax.axis_size("lat") * lax.axis_size("lon") * cells.shape[0]
    pick = (jnp.arange(total, dtype=jnp.int32)[:, None] == wanted[None, :]).astype(jnp.float32)

    def donate(field):
        flat = field.reshape(comps * levels, rows, cols)
        along = jnp.einsum("kij,sj->kis", flat, weight_lon, precision=HIGHEST)
        value = jnp.sum(along * weight_lat.T[None], axis=1)
        return rotate(value.reshape(comps, levels, -1), turn).reshape(comps * levels, -1)

    def receive(given):
        whole = lax.all_gather(given, ("lat", "lon"), axis=1, tiled=True)
        partner = partner_2(whole, "panel", 0)
        return jnp.dot(partner, pick, precision=HIGHEST)

    def section(field):
        up = shift(field[:, :, rows - 2 :, :], "lat", 1)
        down = shift(field[:, :, :2, :], "lat", -1)
        left = shift(field[:, :, :, cols - 2 :], "lon", 1)
        right = shift(field[:, :, :, :2], "lon", -1)
        rim = receive(donate(field)).reshape(comps, levels, -1)
        rim_lat = rim[:, :, :band].reshape(comps, levels, 2, cols)
        rim_lon = jnp.transpose(rim[:, :, band:].reshape(comps, levels, 2, rows), (0, 1, 3, 2))
        up = jnp.where(on_top, rim_lat, up)
        down = jnp.where(on_bottom, rim_lat, down)
        left = jnp.where(on_left, rim_lon, left)
        right = jnp.where(on_right, rim_lon, right)
        return rate(up, field, down, left, right)

    field = state[0]
    section_one = field + time_step * section(field)
    second = section(section_one)
    new_field = 0.5 * field + 0.5 * (section_one + time_step * second)
    return new_field[None]


def solution(mesh):
    in_specs = (
        P("panel", None, None, "lat", "lon"),
        P("panel", "lat", "lon", None),
        P("panel", "lat", "lon", None),
        P("panel", "lat", "lon", None, None),
        P("panel", "lat", "lon", None),
    )
    out_specs = P("panel", None, None, "lat", "lon")
    return jax.shard_map(
        per_device, mesh=mesh, in_specs=in_specs, out_specs=out_specs, check_vma=False
    )
```

profile of v0, /device:TPU:1, one launch (start us, length us, event | category | flops | bytes accessed | tf_op | source)
XLA Modules:
  0.0 83.6 jit_solution(6090372736300227283)
XLA Ops:
  0.0 0.7 broadcast_remainder_fusion
  0.7 0.7 compare_reduce_fusion
  1.4 0.8 fusion.71
  2.2 2.1 %fusion.6 = f32[14,192]{1,0:T(8,128)S(1)} fusion(f32[14,64,128]{2,1,0:T(8,128)} %bitcast.119, f32[64,192]{1,0:T(8,128)S(1)} %select_add_fusion.3, f32[192]{0:T(256)S(1)} %bitcast.153, s32[192]{0:T(256)S(1)} %get-tuple-element.50, f32[192]{0:T(256)S(1)} %broadcast_subtract_fusion.1, s32[192]{0:T(256)S(1)} %get-tuple-element.49), kind=kOutput, calls=%fused_computation.9 | convolution fusion | flops 264705408 | bytes 521728 | tf_op jit(solution)/shard_map/kij,sj->kis/dot_general | solution.py:113
  4.5 23.7 %all-gather = f32[16,192,14]{1,2,0:T(8,128)S(1)} all-gather(f32[1,192,14]{1,2,0:T(8,128)S(1)} %bitcast.145), channel_id=1, replica_groups=mesh['panel'=2,'lat'=4,'lon'=4] {'lat','lon'}, dimensions={0}, use_global_device_ids=true | all-gather | bytes 182784 | tf_op jit(solution)/shard_map/all_gather | solution.py:118
  28.1 0.1 copy.18
  28.3 0.1 reshape.364
  28.4 1.3 %collective-permute-start = (f32[14,3072]{1,0:T(8,128)S(1)}, f32[14,3072]{1,0:T(8,128)S(1)}, u32[]{:S(2)}, u32[]{:S(2)}) collective-permute-start(f32[14,3072]{1,0:T(8,128)S(1)} %bitcast.127), channel_id=1, source_target_pairs={{0,16},{16,0},{1,17},{17,1},{2,18},{18,2},{3,19},{19,3},{4,20},{20... | collective-permute-start | bytes 516104 | tf_op jit(solution)/shard_map/ppermute | solution.py:21
  29.7 0.2 fusion.68
  29.9 2.4 %collective-permute-start.3 = (f32[7,2,64,2]{3,2,1,0:T(8,128)S(1)}, f32[7,2,64,2]{3,2,1,0:T(8,128)S(1)}, u32[]{:S(2)}, u32[]{:S(2)}) collective-permute-start(f32[7,2,64,2]{3,2,1,0:T(8,128)S(1)} %get-tuple-element.36), channel_id=1, source_target_pairs={{1,0},{2,1},{3,2},{5,4},{6,5},{7,6},{9,8},{10,9},{11,10},{13,12},{... | collective-permute-start | bytes 21512 | tf_op jit(solution)/shard_map/ppermute | solution.py:30
  32.3 3.2 %collective-permute-start.4 = (f32[7,2,64,2]{3,2,1,0:T(8,128)S(1)}, f32[7,2,64,2]{3,2,1,0:T(8,128)S(1)}, u32[]{:S(2)}, u32[]{:S(2)}) collective-permute-start(f32[7,2,64,2]{3,2,1,0:T(8,128)S(1)} %get-tuple-element.35), channel_id=1, source_target_pairs={{0,1},{1,2},{2,3},{4,5},{5,6},{6,7},{8,9},{9,10},{10,11},{12,13},{... | collective-permute-start | bytes 21512 | tf_op jit(solution)/shard_map/ppermute | solution.py:30
  35.5 1.3 %collective-permute-start.1 = (f32[7,2,2,128]{3,2,1,0:T(2,128)S(1)}, f32[7,2,2,128]{3,2,1,0:T(2,128)S(1)}, u32[]{:S(2)}, u32[]{:S(2)}) collective-permute-start(f32[7,2,2,128]{3,2,1,0:T(2,128)S(1)} %get-tuple-element.38), channel_id=1, source_target_pairs={{4,0},{8,4},{12,8},{5,1},{9,5},{13,9},{6,2},{10,6},{14,10},{7,3},{... | collective-permute-start | bytes 43016 | tf_op jit(solution)/shard_map/ppermute | solution.py:30
  36.8 4.0 %collective-permute-start.2 = (f32[7,2,2,128]{3,2,1,0:T(2,128)S(1)}, f32[7,2,2,128]{3,2,1,0:T(2,128)S(1)}, u32[]{:S(2)}, u32[]{:S(2)}) collective-permute-start(f32[7,2,2,128]{3,2,1,0:T(2,128)S(1)} %get-tuple-element.37), channel_id=1, source_target_pairs={{0,4},{4,8},{8,12},{1,5},{5,9},{9,13},{2,6},{6,10},{10,14},{3,7},{... | collective-permute-start | bytes 43016 | tf_op jit(solution)/shard_map/ppermute | solution.py:30
  40.9 1.5 %fusion.1 = f32[14,384]{1,0:T(8,128)S(1)} fusion(f32[14,3072]{1,0:T(8,128)S(1)} %collective-permute-done, s32[384]{0:T(512)S(1)} %pad_add_fusion), kind=kOutput, calls=%fused_computation.2 | convolution fusion | flops 199360512 | bytes 195072 | tf_op jit(solution)/shard_map/dot_general | solution.py:120
  42.5 0.2 copy.19
  43.0 0.9 %multiply_add_fusion.2 = (f32[7,2,64,128]{3,2,1,0:T(8,128)S(1)}, f32[7,2,64,128]{3,2,1,0:T(8,128)S(1)}, f32[7,2,64,128]{3,2,1,0:T(8,128)S(1)}) fusion(f32[2,64,128]{2,1,0:T(8,128)S(1)} %get-tuple-element.30, f32[2,64,128]{2,1,0:T(8,128)S(1)} %get-tuple-element.31, f32[7,2,64,128]{3,2,1,0:T(8,128)S(1)} %bitcast.122, ...), kind=kLoop, calls=%fused_computation.74 | loop fusion | flops 2179072 | bytes 2009088 | tf_op jit(solution)/shard_map/add | solution.py:52
  43.9 0.6 fusion.17
  44.7 0.9 %fusion.66 = (f32[7,2,64,2]{3,2,1,0:T(8,128)S(1)}, f32[7,2,64,2]{3,2,1,0:T(8,128)}) fusion(f32[7,2,64,128]{3,2,1,0:T(8,128)S(1)} %get-tuple-element.28), kind=kLoop, calls=%fused_computation.175 | loop fusion | bytes 28672 | tf_op jit(solution)/shard_map/slice | solution.py:125
  45.7 1.0 %fusion.5 = f32[14,192]{1,0:T(8,128)S(1)} fusion(f32[14,64,128]{2,1,0:T(8,128)S(1)} %bitcast_add_fusion, f32[64,192]{1,0:T(8,128)S(1)} %select_add_fusion.3, f32[192]{0:T(256)S(1)} %bitcast.154, s32[192]{0:T(256)S(1)} %get-tuple-element.50, f32[192]{0:T(256)S(1)} %broadcast_subtract_fusion.1, s32[192]{0:T(256)S(1)} %get-tuple-element.49), kind=kOutput, calls=%fused_computation.8 | convolution fusion | flops 264705408 | bytes 521728 | tf_op jit(solution)/shard_map/kij,sj->kis/dot_general | solution.py:113
  46.9 18.7 %all-gather.1 = f32[16,192,14]{1,2,0:T(8,128)S(1)} all-gather(f32[1,192,14]{1,2,0:T(8,128)S(1)} %bitcast.146), channel_id=1, replica_groups=mesh['panel'=2,'lat'=4,'lon'=4] {'lat','lon'}, dimensions={0}, use_global_device_ids=true | all-gather | bytes 182784 | tf_op jit(solution)/shard_map/all_gather | solution.py:118
  65.6 0.1 copy.20
  65.8 0.6 collective-permute-start.5
  66.5 2.3 %collective-permute-start.8 = (f32[7,2,64,2]{3,2,1,0:T(8,128)}, f32[7,2,64,2]{3,2,1,0:T(8,128)S(1)}, u32[]{:S(2)}, u32[]{:S(2)}) collective-permute-start(f32[7,2,64,2]{3,2,1,0:T(8,128)} %get-tuple-element.24), channel_id=1, source_target_pairs={{1,0},{2,1},{3,2},{5,4},{6,5},{7,6},{9,8},{10,9},{11,10},{13,12},{... | collective-permute-start | bytes 21512 | tf_op jit(solution)/shard_map/ppermute | solution.py:30
  68.8 3.2 %collective-permute-start.9 = (f32[7,2,64,2]{3,2,1,0:T(8,128)S(1)}, f32[7,2,64,2]{3,2,1,0:T(8,128)}, u32[]{:S(2)}, u32[]{:S(2)}) collective-permute-start(f32[7,2,64,2]{3,2,1,0:T(8,128)S(1)} %get-tuple-element.23), channel_id=1, source_target_pairs={{0,1},{1,2},{2,3},{4,5},{5,6},{6,7},{8,9},{9,10},{10,11},{12,13},{... | collective-permute-start | bytes 21512 | tf_op jit(solution)/shard_map/ppermute | solution.py:30
  72.1 1.3 %collective-permute-start.6 = (f32[7,2,2,128]{3,2,1,0:T(2,128)S(1)}, f32[7,2,2,128]{3,2,1,0:T(2,128)S(1)}, u32[]{:S(2)}, u32[]{:S(2)}) collective-permute-start(f32[7,2,2,128]{3,2,1,0:T(2,128)S(1)} %get-tuple-element.26), channel_id=1, source_target_pairs={{4,0},{8,4},{12,8},{5,1},{9,5},{13,9},{6,2},{10,6},{14,10},{7,3},{... | collective-permute-start | bytes 43016 | tf_op jit(solution)/shard_map/ppermute | solution.py:30
  73.4 4.6 %collective-permute-start.7 = (f32[7,2,2,128]{3,2,1,0:T(2,128)S(1)}, f32[7,2,2,128]{3,2,1,0:T(2,128)}, u32[]{:S(2)}, u32[]{:S(2)}) collective-permute-start(f32[7,2,2,128]{3,2,1,0:T(2,128)S(1)} %get-tuple-element.25), channel_id=1, source_target_pairs={{0,4},{4,8},{8,12},{1,5},{5,9},{9,13},{2,6},{6,10},{10,14},{3,7},{... | collective-permute-start | bytes 43016 | tf_op jit(solution)/shard_map/ppermute | solution.py:30
  78.0 1.5 %fusion = f32[14,384]{1,0:T(8,128)S(1)} fusion(f32[14,3072]{1,0:T(8,128)S(1)} %collective-permute-done.5, s32[384]{0:T(512)S(1)} %pad_add_fusion), kind=kOutput, calls=%fused_computation.1 | convolution fusion | flops 199360512 | bytes 195072 | tf_op jit(solution)/shard_map/dot_general | solution.py:120
  79.6 0.2 copy.21
  79.8 1.1 %bitcast_select_fusion = (f32[7,2,64,2]{3,2,1,0:T(8,128)S(1)}, f32[7,2,64,2]{3,2,1,0:T(8,128)S(1)}) fusion(f32[7,2,64,2]{3,2,1,0:T(8,128)} %collective-permute-done.9, f32[7,2,2,64]{2,3,1,0:T(8,128)S(1)} %copy.21, pred[]{:T(512)S(6)} %eq.104, f32[7,2,64,2]{3,2,1,0:T(8,128)S(1)} %collective-permute-done.8, pred[]{:T(512)S(6)} %eq.107), kind=kLoop, calls=%fused_computation.67 | loop fusion | flops 3584 | bytes 35842 | tf_op jit(solution)/shard_map/jit(_where)/select_n | solution.py:132
  81.1 0.5 fusion.20
  81.6 0.9 %multiply_add_fusion = (f32[7,2,64,128]{3,2,1,0:T(8,128)S(1)}, f32[7,2,64,128]{3,2,1,0:T(8,128)S(1)}, f32[7,2,64,128]{3,2,1,0:T(8,128)S(1)}) fusion(f32[2,64,128]{2,1,0:T(8,128)S(1)} %get-tuple-element.20, f32[2,64,128]{2,1,0:T(8,128)S(1)} %get-tuple-element.18, f32[7,2,64,128]{3,2,1,0:T(8,128)S(1)} %get-tuple-element.28, ...), kind=kLoop, calls=%fused_computation.72 | loop fusion | flops 2179072 | bytes 2009088 | tf_op jit(solution)/shard_map/add | solution.py:52
  82.7 0.9 %fusion.32 = f32[1,7,2,64,128]{4,3,2,1,0:T(8,128)} fusion(f32[1,7,2,64,128]{4,3,2,1,0:T(8,128)S(1)} %copy-done, f32[1,1,2,64,128]{4,3,2,1,0:T(8,128)S(1)} %bitcast.126, f32[1,3,2,64,128]{4,3,2,1,0:T(8,128)S(1)} %bitcast.124, f32[1,2,2,64,128]{4,3,2,1,0:T(8,128)S(1)} %get-tuple-element.40, f32[1,1,2,64,128]{4,3,2,1,0:T(8,128)S(1)} %bitcast.125, ...), kind=kLoop, calls=%fused_computation.64 | loop fusion | flops 1376256 | bytes 1835008 | tf_op jit(solution)/shard_map/add | solution.py:139
  (69 shorter events, 1.4 us)
Async XLA Ops:
  0.0 4.3 %copy-start.2 = (f32[1,1,1,192]{3,2,1,0:T(1,128)S(1)}, f32[1,1,1,192]{3,2,1,0:T(1,128)}, u32[]{:S(2)}) copy-start(f32[1,1,1,192]{3,2,1,0:T(1,128)} %param.9) | copy-start | bytes 2308
  28.1 1.6 %copy-start = (f32[1,7,2,64,128]{4,3,2,1,0:T(8,128)S(1)}, f32[1,7,2,64,128]{4,3,2,1,0:T(8,128)}, u32[]{:S(2)}) copy-start(f32[1,7,2,64,128]{4,3,2,1,0:T(8,128)} %param.5) | copy-start | bytes 1376260
  28.4 12.5 %collective-permute-start = (f32[14,3072]{1,0:T(8,128)S(1)}, f32[14,3072]{1,0:T(8,128)S(1)}, u32[]{:S(2)}, u32[]{:S(2)}) collective-permute-start(f32[14,3072]{1,0:T(8,128)S(1)} %bitcast.127), channel_id=1, source_target_pairs={{0,16},{16,0},{1,17},{17,1},{2,18},{18,2},{3,19},{19,3},{4,20},{20... | collective-permute-start | bytes 516104 | tf_op jit(solution)/shard_map/ppermute | solution.py:21
  29.9 11.0 %copy-start.1 = (s32[1,1,1,768]{3,2,1,0:T(1,128)S(1)}, s32[1,1,1,768]{3,2,1,0:T(1,128)}, u32[]{:S(2)}) copy-start(s32[1,1,1,768]{3,2,1,0:T(1,128)} %param.6) | copy-start | bytes 9220
  29.9 12.9 %collective-permute-start.3 = (f32[7,2,64,2]{3,2,1,0:T(8,128)S(1)}, f32[7,2,64,2]{3,2,1,0:T(8,128)S(1)}, u32[]{:S(2)}, u32[]{:S(2)}) collective-permute-start(f32[7,2,64,2]{3,2,1,0:T(8,128)S(1)} %get-tuple-element.36), channel_id=1, source_target_pairs={{1,0},{2,1},{3,2},{5,4},{6,5},{7,6},{9,8},{10,9},{11,10},{13,12},{... | collective-permute-start | bytes 21512 | tf_op jit(solution)/shard_map/ppermute | solution.py:30
  32.3 10.5 %collective-permute-start.4 = (f32[7,2,64,2]{3,2,1,0:T(8,128)S(1)}, f32[7,2,64,2]{3,2,1,0:T(8,128)S(1)}, u32[]{:S(2)}, u32[]{:S(2)}) collective-permute-start(f32[7,2,64,2]{3,2,1,0:T(8,128)S(1)} %get-tuple-element.35), channel_id=1, source_target_pairs={{0,1},{1,2},{2,3},{4,5},{5,6},{6,7},{8,9},{9,10},{10,11},{12,13},{... | collective-permute-start | bytes 21512 | tf_op jit(solution)/shard_map/ppermute | solution.py:30
  35.5 7.5 %collective-permute-start.1 = (f32[7,2,2,128]{3,2,1,0:T(2,128)S(1)}, f32[7,2,2,128]{3,2,1,0:T(2,128)S(1)}, u32[]{:S(2)}, u32[]{:S(2)}) collective-permute-start(f32[7,2,2,128]{3,2,1,0:T(2,128)S(1)} %get-tuple-element.38), channel_id=1, source_target_pairs={{4,0},{8,4},{12,8},{5,1},{9,5},{13,9},{6,2},{10,6},{14,10},{7,3},{... | collective-permute-start | bytes 43016 | tf_op jit(solution)/shard_map/ppermute | solution.py:30
  36.8 6.2 %collective-permute-start.2 = (f32[7,2,2,128]{3,2,1,0:T(2,128)S(1)}, f32[7,2,2,128]{3,2,1,0:T(2,128)S(1)}, u32[]{:S(2)}, u32[]{:S(2)}) collective-permute-start(f32[7,2,2,128]{3,2,1,0:T(2,128)S(1)} %get-tuple-element.37), channel_id=1, source_target_pairs={{0,4},{4,8},{8,12},{1,5},{5,9},{9,13},{2,6},{6,10},{10,14},{3,7},{... | collective-permute-start | bytes 43016 | tf_op jit(solution)/shard_map/ppermute | solution.py:30
  65.8 12.1 %collective-permute-start.5 = (f32[14,3072]{1,0:T(8,128)S(1)}, f32[14,3072]{1,0:T(8,128)S(1)}, u32[]{:S(2)}, u32[]{:S(2)}) collective-permute-start(f32[14,3072]{1,0:T(8,128)S(1)} %bitcast.128), channel_id=1, source_target_pairs={{0,16},{16,0},{1,17},{17,1},{2,18},{18,2},{3,19},{19,3},{4,20},{20... | collective-permute-start | bytes 516104 | tf_op jit(solution)/shard_map/ppermute | solution.py:21
  66.5 13.3 %collective-permute-start.8 = (f32[7,2,64,2]{3,2,1,0:T(8,128)}, f32[7,2,64,2]{3,2,1,0:T(8,128)S(1)}, u32[]{:S(2)}, u32[]{:S(2)}) collective-permute-start(f32[7,2,64,2]{3,2,1,0:T(8,128)} %get-tuple-element.24), channel_id=1, source_target_pairs={{1,0},{2,1},{3,2},{5,4},{6,5},{7,6},{9,8},{10,9},{11,10},{13,12},{... | collective-permute-start | bytes 21512 | tf_op jit(solution)/shard_map/ppermute | solution.py:30
  68.8 11.0 %collective-permute-start.9 = (f32[7,2,64,2]{3,2,1,0:T(8,128)S(1)}, f32[7,2,64,2]{3,2,1,0:T(8,128)}, u32[]{:S(2)}, u32[]{:S(2)}) collective-permute-start(f32[7,2,64,2]{3,2,1,0:T(8,128)S(1)} %get-tuple-element.23), channel_id=1, source_target_pairs={{0,1},{1,2},{2,3},{4,5},{5,6},{6,7},{8,9},{9,10},{10,11},{12,13},{... | collective-permute-start | bytes 21512 | tf_op jit(solution)/shard_map/ppermute | solution.py:30
  72.1 9.0 %collective-permute-start.6 = (f32[7,2,2,128]{3,2,1,0:T(2,128)S(1)}, f32[7,2,2,128]{3,2,1,0:T(2,128)S(1)}, u32[]{:S(2)}, u32[]{:S(2)}) collective-permute-start(f32[7,2,2,128]{3,2,1,0:T(2,128)S(1)} %get-tuple-element.26), channel_id=1, source_target_pairs={{4,0},{8,4},{12,8},{5,1},{9,5},{13,9},{6,2},{10,6},{14,10},{7,3},{... | collective-permute-start | bytes 43016 | tf_op jit(solution)/shard_map/ppermute | solution.py:30
  73.4 7.7 %collective-permute-start.7 = (f32[7,2,2,128]{3,2,1,0:T(2,128)S(1)}, f32[7,2,2,128]{3,2,1,0:T(2,128)}, u32[]{:S(2)}, u32[]{:S(2)}) collective-permute-start(f32[7,2,2,128]{3,2,1,0:T(2,128)S(1)} %get-tuple-element.25), channel_id=1, source_target_pairs={{0,4},{4,8},{8,12},{1,5},{5,9},{9,13},{2,6},{6,10},{10,14},{3,7},{... | collective-permute-start | bytes 43016 | tf_op jit(solution)/shard_map/ppermute | solution.py:30
where the time goes:
time: 84.2 us; the launch traced here: 83.6 us
  blocking collectives  42.4 us (50%)
  starting transfers between devices  24.2 us (29%)
  other arithmetic  7.14 us (8%)
  matrix products  6.06 us (7%)
  local copies, waits for them, and re-layouts  3.29 us (4%)
    all_gather x2, blocking collectives, receive(): whole = lax.all_gather(given, ('lat', 'lon'), axis=1, tiled=True)  42.4 us
    ppermute x8, starting transfers between devices, shift(): return lax.ppermute(value, axis, route)  22.3 us
    dot_general x2, matrix products, donate(): along = jnp.einsum('kij,sj->kis', flat, weight_lon, precision=HIGHEST)  3.09 us
    dot_general x2, matrix products, receive(): return jnp.dot(partner, pick, precision=HIGHEST)  2.97 us
    ppermute x2, starting transfers between devices, partner_2(): return lax.ppermute(block, axis, route)  1.94 us
    add x2, other arithmetic, rate(): adv_b = middle[4:5] * d_lat + middle[5:6] * d_lon  1.8 us
  transfers between devices with their start and end apart: 10, of which 0 were waited for; matrix products, arithmetic and copies ran while one was open for 6% of the time, Pallas kernels for 0%

commit v1 on v0

--- a/solution.py
+++ b/solution.py
@@ -115,7 +115,31 @@
         return rotate(value.reshape(comps, levels, -1), turn).reshape(comps * levels, -1)
 
     def receive(given):
-        whole = lax.all_gather(given, ("lat", "lon"), axis=1, tiled=True)
+        ways, here, step_2 = (
+            lax.axis_size(("lat", "lon")),
+            lax.axis_index(("lat", "lon")),
+            given.shape[1],
+        )
+        dims = [n * ways if d == 1 else n for d, n in enumerate(given.shape)]
+        full = lax.dynamic_update_slice_in_dim(
+            jnp.zeros(dims, given.dtype), given, here * step_2, axis=1
+        )
+        going_up = going_down = given
+        for far in range(1, ways // 2 + 1):
+            going_up = lax.ppermute(
+                going_up, ("lat", "lon"), [(d, (d + 1) % ways) for d in range(ways)]
+            )
+            full = lax.dynamic_update_slice_in_dim(
+                full, going_up, (here - far) % ways * step_2, axis=1
+            )
+            if 2 * far < ways:
+                going_down = lax.ppermute(
+                    going_down, ("lat", "lon"), [(d, (d - 1) % ways) for d in range(ways)]
+                )
+                full = lax.dynamic_update_slice_in_dim(
+                    full, going_down, (here + far) % ways * step_2, axis=1
+                )
+        whole = full
         partner = partner_2(whole, "panel", 0)
         return jnp.dot(partner, pick, precision=HIGHEST)
 

time: 84.2 us -> 138 us (1.64); the launches traced: 83.6 us -> 135 us
  starting transfers between devices: 24.2 us -> 90.7 us
  blocking collectives: 42.4 us -> 0 us
  waiting for transfers between devices: 0.03 us -> 15.2 us
  local copies, waits for them, and re-layouts: 3.29 us -> 14.6 us
    ppermute x0 -> x30, starting transfers between devices: none -> 60.5 us  [the longest x14 49.8 us: receive(): lax.ppermute(going_down, ('lat', 'lon'), [(d, (d - 1) % ways) for d in ra...]
    all_gather x2 -> x0, blocking collectives: 42.4 us -> none  [receive(): whole = lax.all_gather(given, ('lat', 'lon'), axis=1, tiled=True)]
    dynamic_update_slice x0 -> x32, local copies, waits for them, and re-layouts: none -> 12.6 us  [the longest x16 6.22 us: receive(): lax.dynamic_update_slice_in_dim(full, going_up, (here - far) % ways * ste...]
    ppermute x0 -> x30, waiting for transfers between devices: none -> 9.06 us  [the longest x16 7.19 us: receive(): lax.ppermute(going_up, ('lat', 'lon'), [(d, (d + 1) % ways) for d in rang...]
    ppermute x2, waiting for transfers between devices: 0.01 us -> 6.08 us  [partner_2(): return lax.ppermute(block, axis, route)]
    ppermute x8, starting transfers between devices: 22.3 us -> 26.6 us  [shift(): return lax.ppermute(value, axis, route)]
    ppermute x2, starting transfers between devices: 1.94 us -> 3.61 us  [partner_2(): return lax.ppermute(block, axis, route)]
  transfers between devices with their start and end apart: 10 -> 40, of which waited for: 0 -> 22; matrix products, arithmetic and copies ran while one was open for 6% -> 13% of each run, Pallas kernels for 0% -> 0%
where the time goes in v1:
time: 138 us; the launch traced here: 135 us
  starting transfers between devices  90.7 us (66%)
  waiting for transfers between devices  15.2 us (11%)
  local copies, waits for them, and re-layouts  14.6 us (11%)
  other arithmetic  7.91 us (6%)
  matrix products  6.06 us (4%)
    ppermute x14, starting transfers between devices, receive(): lax.ppermute(going_down, ('lat', 'lon'), [(d, (d - 1) % ways) for d in ra...  49.8 us
    ppermute x8, starting transfers between devices, shift(): return lax.ppermute(value, axis, route)  26.6 us
    ppermute x16, starting transfers between devices, receive(): lax.ppermute(going_up, ('lat', 'lon'), [(d, (d + 1) % ways) for d in rang...  10.7 us
    ppermute x16, waiting for transfers between devices, receive(): lax.ppermute(going_up, ('lat', 'lon'), [(d, (d + 1) % ways) for d in rang...  7.19 us
    dynamic_update_slice x16, local copies, waits for them, and re-layouts, receive(): lax.dynamic_update_slice_in_dim(full, going_up, (here - far) % ways * ste...  6.22 us
    ppermute x2, waiting for transfers between devices, partner_2(): return lax.ppermute(block, axis, route)  6.08 us
    dynamic_update_slice x14, local copies, waits for them, and re-layouts, receive(): lax.dynamic_update_slice_in_dim(full, going_down, (here + far) % ways * s...  5.42 us
    ppermute x2, starting transfers between devices, partner_2(): return lax.ppermute(block, axis, route)  3.61 us
  transfers between devices with their start and end apart: 40, of which 22 were waited for; matrix products, arithmetic and copies ran while one was open for 13% of the time, Pallas kernels for 0%

profile of v1, /device:TPU:1, one launch (start us, length us, event | category | flops | bytes accessed | tf_op | source)
XLA Modules:
  0.0 135.3 jit_solution(17869142375187274265)
XLA Ops:
  2.3 2.1 %fusion.6 = f32[14,192]{1,0:T(8,128)S(1)} fusion(f32[14,64,128]{2,1,0:T(8,128)} %bitcast.107, f32[64,192]{1,0:T(8,128)S(1)} %select_add_fusion.3, f32[192]{0:T(256)S(1)} %bitcast.137, s32[192]{0:T(256)S(1)} %get-tuple-element.50, f32[192]{0:T(256)S(1)} %broadcast_subtract_fusion.1, s32[192]{0:T(256)S(1)} %get-tuple-element.49), kind=kOutput, calls=%fused_computation.9 | convolution fusion | flops 264705408 | bytes 521728 | tf_op jit(solution)/shard_map/kij,sj->kis/dot_general | solution.py:113
  4.5 2.7 %collective-permute-start = (f32[14,192]{1,0:T(8,128)S(1)}, f32[14,192]{1,0:T(8,128)S(1)}, u32[]{:S(2)}, u32[]{:S(2)}) collective-permute-start(f32[14,192]{1,0:T(8,128)S(1)} %reshape.355), channel_id=1, source_target_pairs={{0,1},{1,2},{2,3},{3,4},{4,5},{5,6},{6,7},{7,8},{8,9},{9,10},{10,1... | collective-permute-start | bytes 32264 | tf_op jit(solution)/shard_map/ppermute | solution.py:129
  8.0 2.3 %collective-permute-start.2 = (f32[14,192]{1,0:T(8,128)S(1)}, f32[14,192]{1,0:T(8,128)S(1)}, u32[]{:S(2)}, u32[]{:S(2)}) collective-permute-start(f32[14,192]{1,0:T(8,128)S(1)} %collective-permute-done), channel_id=1, source_target_pairs={{0,1},{1,2},{2,3},{3,4},{4,5},{5,6},{6,7},{7,8},{8,9},{9,10},{10,1... | collective-permute-start | bytes 32264 | tf_op jit(solution)/shard_map/ppermute | solution.py:129
  12.1 1.4 %collective-permute-start.4 = (f32[14,192]{1,0:T(8,128)S(1)}, f32[14,192]{1,0:T(8,128)S(1)}, u32[]{:S(2)}, u32[]{:S(2)}) collective-permute-start(f32[14,192]{1,0:T(8,128)S(1)} %collective-permute-done.2), channel_id=1, source_target_pairs={{0,1},{1,2},{2,3},{3,4},{4,5},{5,6},{6,7},{7,8},{8,9},{9,10},{10,1... | collective-permute-start | bytes 32264 | tf_op jit(solution)/shard_map/ppermute | solution.py:129
  13.8 3.6 %collective-permute-start.5 = (f32[14,192]{1,0:T(8,128)S(1)}, f32[14,192]{1,0:T(8,128)S(1)}, u32[]{:S(2)}, u32[]{:S(2)}) collective-permute-start(f32[14,192]{1,0:T(8,128)S(1)} %collective-permute-done.3), channel_id=1, source_target_pairs={{0,15},{1,0},{2,1},{3,2},{4,3},{5,4},{6,5},{7,6},{8,7},{9,8},{10,9... | collective-permute-start | bytes 32264 | tf_op jit(solution)/shard_map/ppermute | solution.py:136
  18.2 7.1 %collective-permute-start.18 = (f32[7,2,64,2]{3,2,1,0:T(8,128)S(1)}, f32[7,2,64,2]{3,2,1,0:T(8,128)S(1)}, u32[]{:S(2)}, u32[]{:S(2)}) collective-permute-start(f32[7,2,64,2]{3,2,1,0:T(8,128)S(1)} %get-tuple-element.36), channel_id=1, source_target_pairs={{1,0},{2,1},{3,2},{5,4},{6,5},{7,6},{9,8},{10,9},{11,10},{13,12},{... | collective-permute-start | bytes 21512 | tf_op jit(solution)/shard_map/ppermute | solution.py:30
  25.3 1.9 %collective-permute-start.19 = (f32[7,2,64,2]{3,2,1,0:T(8,128)S(1)}, f32[7,2,64,2]{3,2,1,0:T(8,128)S(1)}, u32[]{:S(2)}, u32[]{:S(2)}) collective-permute-start(f32[7,2,64,2]{3,2,1,0:T(8,128)S(1)} %get-tuple-element.35), channel_id=1, source_target_pairs={{0,1},{1,2},{2,3},{4,5},{5,6},{6,7},{8,9},{9,10},{10,11},{12,13},{... | collective-permute-start | bytes 21512 | tf_op jit(solution)/shard_map/ppermute | solution.py:30
  27.8 1.2 collective-permute-start.8
  29.1 1.3 collective-permute-start.16
  30.5 1.5 %collective-permute-start.9 = (f32[14,192]{1,0:T(8,128)S(1)}, f32[14,192]{1,0:T(8,128)S(1)}, u32[]{:S(2)}, u32[]{:S(2)}) collective-permute-start(f32[14,192]{1,0:T(8,128)S(1)} %collective-permute-done.7), channel_id=1, source_target_pairs={{0,15},{1,0},{2,1},{3,2},{4,3},{5,4},{6,5},{7,6},{8,7},{9,8},{10,9... | collective-permute-start | bytes 32264 | tf_op jit(solution)/shard_map/ppermute | solution.py:136
  32.8 2.5 %collective-permute-start.10 = (f32[14,192]{1,0:T(8,128)S(1)}, f32[14,192]{1,0:T(8,128)S(1)}, u32[]{:S(2)}, u32[]{:S(2)}) collective-permute-start(f32[14,192]{1,0:T(8,128)S(1)} %collective-permute-done.8), channel_id=1, source_target_pairs={{0,1},{1,2},{2,3},{3,4},{4,5},{5,6},{6,7},{7,8},{8,9},{9,10},{10,1... | collective-permute-start | bytes 32264 | tf_op jit(solution)/shard_map/ppermute | solution.py:129
  35.3 2.5 %collective-permute-start.11 = (f32[14,192]{1,0:T(8,128)S(1)}, f32[14,192]{1,0:T(8,128)S(1)}, u32[]{:S(2)}, u32[]{:S(2)}) collective-permute-start(f32[14,192]{1,0:T(8,128)S(1)} %collective-permute-done.9), channel_id=1, source_target_pairs={{0,15},{1,0},{2,1},{3,2},{4,3},{5,4},{6,5},{7,6},{8,7},{9,8},{10,9... | collective-permute-start | bytes 32264 | tf_op jit(solution)/shard_map/ppermute | solution.py:136
  38.7 5.0 %collective-permute-start.13 = (f32[14,192]{1,0:T(8,128)S(1)}, f32[14,192]{1,0:T(8,128)S(1)}, u32[]{:S(2)}, u32[]{:S(2)}) collective-permute-start(f32[14,192]{1,0:T(8,128)S(1)} %collective-permute-done.11), channel_id=1, source_target_pairs={{0,15},{1,0},{2,1},{3,2},{4,3},{5,4},{6,5},{7,6},{8,7},{9,8},{10,9... | collective-permute-start | bytes 32264 | tf_op jit(solution)/shard_map/ppermute | solution.py:136
  49.4 1.5 %collective-permute-start.17 = (f32[7,2,2,128]{3,2,1,0:T(2,128)S(1)}, f32[7,2,2,128]{3,2,1,0:T(2,128)S(1)}, u32[]{:S(2)}, u32[]{:S(2)}) collective-permute-start(f32[7,2,2,128]{3,2,1,0:T(2,128)S(1)} %get-tuple-element.37), channel_id=1, source_target_pairs={{0,4},{4,8},{8,12},{1,5},{5,9},{9,13},{2,6},{6,10},{10,14},{3,7},{... | collective-permute-start | bytes 43016 | tf_op jit(solution)/shard_map/ppermute | solution.py:30
  51.8 1.8 %collective-permute-start.15 = (f32[14,3072]{1,0:T(8,128)S(1)}, f32[14,3072]{1,0:T(8,128)S(1)}, u32[]{:S(2)}, u32[]{:S(2)}) collective-permute-start(f32[14,3072]{1,0:T(8,128)S(1)} %dynamic_update_slice.111), channel_id=1, source_target_pairs={{0,16},{16,0},{1,17},{17,1},{2,18},{18,2},{3,19},{19,3},{4,20},{20... | collective-permute-start | bytes 516104 | tf_op jit(solution)/shard_map/ppermute | solution.py:21
  53.6 3.0 %collective-permute-done.15 = f32[14,3072]{1,0:T(8,128)S(1)} collective-permute-done((f32[14,3072]{1,0:T(8,128)S(1)}, f32[14,3072]{1,0:T(8,128)S(1)}, u32[]{:S(2)}, u32[]{:S(2)}) %collective-permute-start.15) | collective-permute-done | bytes 172064 | tf_op jit(solution)/shard_map/ppermute | solution.py:21
  56.6 1.5 %fusion.1 = f32[14,384]{1,0:T(8,128)S(1)} fusion(f32[14,3072]{1,0:T(8,128)S(1)} %collective-permute-done.15, s32[384]{0:T(512)S(1)} %pad_add_fusion), kind=kOutput, calls=%fused_computation.2 | convolution fusion | flops 199360512 | bytes 195072 | tf_op jit(solution)/shard_map/dot_general | solution.py:144
  61.7 5.3 %collective-permute-start.21 = (f32[14,192]{1,0:T(8,128)S(1)}, f32[14,192]{1,0:T(8,128)S(1)}, u32[]{:S(2)}, u32[]{:S(2)}) collective-permute-start(f32[14,192]{1,0:T(8,128)S(1)} %reshape.359), channel_id=1, source_target_pairs={{0,15},{1,0},{2,1},{3,2},{4,3},{5,4},{6,5},{7,6},{8,7},{9,8},{10,9... | collective-permute-start | bytes 32264 | tf_op jit(solution)/shard_map/ppermute | solution.py:136
  67.9 5.0 %collective-permute-start.23 = (f32[14,192]{1,0:T(8,128)S(1)}, f32[14,192]{1,0:T(8,128)S(1)}, u32[]{:S(2)}, u32[]{:S(2)}) collective-permute-start(f32[14,192]{1,0:T(8,128)S(1)} %collective-permute-done.21), channel_id=1, source_target_pairs={{0,15},{1,0},{2,1},{3,2},{4,3},{5,4},{6,5},{7,6},{8,7},{9,8},{10,9... | collective-permute-start | bytes 32264 | tf_op jit(solution)/shard_map/ppermute | solution.py:136
  73.7 5.0 %collective-permute-start.25 = (f32[14,192]{1,0:T(8,128)S(1)}, f32[14,192]{1,0:T(8,128)S(1)}, u32[]{:S(2)}, u32[]{:S(2)}) collective-permute-start(f32[14,192]{1,0:T(8,128)S(1)} %collective-permute-done.23), channel_id=1, source_target_pairs={{0,15},{1,0},{2,1},{3,2},{4,3},{5,4},{6,5},{7,6},{8,7},{9,8},{10,9... | collective-permute-start | bytes 32264 | tf_op jit(solution)/shard_map/ppermute | solution.py:136
  79.6 5.0 %collective-permute-start.27 = (f32[14,192]{1,0:T(8,128)S(1)}, f32[14,192]{1,0:T(8,128)S(1)}, u32[]{:S(2)}, u32[]{:S(2)}) collective-permute-start(f32[14,192]{1,0:T(8,128)S(1)} %collective-permute-done.25), channel_id=1, source_target_pairs={{0,15},{1,0},{2,1},{3,2},{4,3},{5,4},{6,5},{7,6},{8,7},{9,8},{10,9... | collective-permute-start | bytes 32264 | tf_op jit(solution)/shard_map/ppermute | solution.py:136
  85.4 5.0 %collective-permute-start.29 = (f32[14,192]{1,0:T(8,128)S(1)}, f32[14,192]{1,0:T(8,128)S(1)}, u32[]{:S(2)}, u32[]{:S(2)}) collective-permute-start(f32[14,192]{1,0:T(8,128)S(1)} %collective-permute-done.27), channel_id=1, source_target_pairs={{0,15},{1,0},{2,1},{3,2},{4,3},{5,4},{6,5},{7,6},{8,7},{9,8},{10,9... | collective-permute-start | bytes 32264 | tf_op jit(solution)/shard_map/ppermute | solution.py:136
  91.3 5.0 %collective-permute-start.31 = (f32[14,192]{1,0:T(8,128)S(1)}, f32[14,192]{1,0:T(8,128)S(1)}, u32[]{:S(2)}, u32[]{:S(2)}) collective-permute-start(f32[14,192]{1,0:T(8,128)S(1)} %collective-permute-done.29), channel_id=1, source_target_pairs={{0,15},{1,0},{2,1},{3,2},{4,3},{5,4},{6,5},{7,6},{8,7},{9,8},{10,9... | collective-permute-start | bytes 32264 | tf_op jit(solution)/shard_map/ppermute | solution.py:136
  97.2 5.2 %collective-permute-start.33 = (f32[14,192]{1,0:T(8,128)S(1)}, f32[14,192]{1,0:T(8,128)S(1)}, u32[]{:S(2)}, u32[]{:S(2)}) collective-permute-start(f32[14,192]{1,0:T(8,128)S(1)} %collective-permute-done.31), channel_id=1, source_target_pairs={{0,15},{1,0},{2,1},{3,2},{4,3},{5,4},{6,5},{7,6},{8,7},{9,8},{10,9... | collective-permute-start | bytes 32264 | tf_op jit(solution)/shard_map/ppermute | solution.py:136
  103.3 7.0 %collective-permute-start.38 = (f32[7,2,64,2]{3,2,1,0:T(8,128)S(1)}, f32[7,2,64,2]{3,2,1,0:T(8,128)S(1)}, u32[]{:S(2)}, u32[]{:S(2)}) collective-permute-start(f32[7,2,64,2]{3,2,1,0:T(8,128)S(1)} %get-tuple-element.24), channel_id=1, source_target_pairs={{1,0},{2,1},{3,2},{5,4},{6,5},{7,6},{9,8},{10,9},{11,10},{13,12},{... | collective-permute-start | bytes 21512 | tf_op jit(solution)/shard_map/ppermute | solution.py:30
  110.3 1.9 %collective-permute-start.39 = (f32[7,2,64,2]{3,2,1,0:T(8,128)S(1)}, f32[7,2,64,2]{3,2,1,0:T(8,128)}, u32[]{:S(2)}, u32[]{:S(2)}) collective-permute-start(f32[7,2,64,2]{3,2,1,0:T(8,128)S(1)} %get-tuple-element.23), channel_id=1, source_target_pairs={{0,1},{1,2},{2,3},{4,5},{5,6},{6,7},{8,9},{9,10},{10,11},{12,13},{... | collective-permute-start | bytes 21512 | tf_op jit(solution)/shard_map/ppermute | solution.py:30
  112.3 1.3 collective-permute-start.36
  118.8 4.6 %collective-permute-start.37 = (f32[7,2,2,128]{3,2,1,0:T(2,128)S(1)}, f32[7,2,2,128]{3,2,1,0:T(2,128)}, u32[]{:S(2)}, u32[]{:S(2)}) collective-permute-start(f32[7,2,2,128]{3,2,1,0:T(2,128)S(1)} %get-tuple-element.25), channel_id=1, source_target_pairs={{0,4},{4,8},{8,12},{1,5},{5,9},{9,13},{2,6},{6,10},{10,14},{3,7},{... | collective-permute-start | bytes 43016 | tf_op jit(solution)/shard_map/ppermute | solution.py:30
  124.0 1.8 %collective-permute-start.35 = (f32[14,3072]{1,0:T(8,128)S(1)}, f32[14,3072]{1,0:T(8,128)S(1)}, u32[]{:S(2)}, u32[]{:S(2)}) collective-permute-start(f32[14,3072]{1,0:T(8,128)S(1)} %dynamic_update_slice.127), channel_id=1, source_target_pairs={{0,16},{16,0},{1,17},{17,1},{2,18},{18,2},{3,19},{19,3},{4,20},{20... | collective-permute-start | bytes 516104 | tf_op jit(solution)/shard_map/ppermute | solution.py:21
  125.9 3.0 %collective-permute-done.35 = f32[14,3072]{1,0:T(8,128)S(1)} collective-permute-done((f32[14,3072]{1,0:T(8,128)S(1)}, f32[14,3072]{1,0:T(8,128)S(1)}, u32[]{:S(2)}, u32[]{:S(2)}) %collective-permute-start.35) | collective-permute-done | bytes 172064 | tf_op jit(solution)/shard_map/ppermute | solution.py:21
  128.9 1.5 %fusion = f32[14,384]{1,0:T(8,128)S(1)} fusion(f32[14,3072]{1,0:T(8,128)S(1)} %collective-permute-done.35, s32[384]{0:T(512)S(1)} %pad_add_fusion), kind=kOutput, calls=%fused_computation.1 | convolution fusion | flops 199360512 | bytes 195072 | tf_op jit(solution)/shard_map/dot_general | solution.py:144
  130.8 1.1 bitcast_select_fusion
  (157 shorter events, 33.8 us)
Async XLA Ops:
  12.1 5.9 %collective-permute-start.4 = (f32[14,192]{1,0:T(8,128)S(1)}, f32[14,192]{1,0:T(8,128)S(1)}, u32[]{:S(2)}, u32[]{:S(2)}) collective-permute-start(f32[14,192]{1,0:T(8,128)S(1)} %collective-permute-done.2), channel_id=1, source_target_pairs={{0,1},{1,2},{2,3},{3,4},{4,5},{5,6},{6,7},{7,8},{8,9},{9,10},{10,1... | collective-permute-start | bytes 32264 | tf_op jit(solution)/shard_map/ppermute | solution.py:129
  13.8 13.4 %collective-permute-start.5 = (f32[14,192]{1,0:T(8,128)S(1)}, f32[14,192]{1,0:T(8,128)S(1)}, u32[]{:S(2)}, u32[]{:S(2)}) collective-permute-start(f32[14,192]{1,0:T(8,128)S(1)} %collective-permute-done.3), channel_id=1, source_target_pairs={{0,15},{1,0},{2,1},{3,2},{4,3},{5,4},{6,5},{7,6},{8,7},{9,8},{10,9... | collective-permute-start | bytes 32264 | tf_op jit(solution)/shard_map/ppermute | solution.py:136
  18.0 9.8 %collective-permute-start.6 = (f32[14,192]{1,0:T(8,128)S(1)}, f32[14,192]{1,0:T(8,128)S(1)}, u32[]{:S(2)}, u32[]{:S(2)}) collective-permute-start(f32[14,192]{1,0:T(8,128)S(1)} %collective-permute-done.4), channel_id=1, source_target_pairs={{0,1},{1,2},{2,3},{3,4},{4,5},{5,6},{6,7},{7,8},{8,9},{9,10},{10,1... | collective-permute-start | bytes 32264 | tf_op jit(solution)/shard_map/ppermute | solution.py:129
  18.2 40.3 %collective-permute-start.18 = (f32[7,2,64,2]{3,2,1,0:T(8,128)S(1)}, f32[7,2,64,2]{3,2,1,0:T(8,128)S(1)}, u32[]{:S(2)}, u32[]{:S(2)}) collective-permute-start(f32[7,2,64,2]{3,2,1,0:T(8,128)S(1)} %get-tuple-element.36), channel_id=1, source_target_pairs={{1,0},{2,1},{3,2},{5,4},{6,5},{7,6},{9,8},{10,9},{11,10},{13,12},{... | collective-permute-start | bytes 21512 | tf_op jit(solution)/shard_map/ppermute | solution.py:30
  25.3 33.2 %collective-permute-start.19 = (f32[7,2,64,2]{3,2,1,0:T(8,128)S(1)}, f32[7,2,64,2]{3,2,1,0:T(8,128)S(1)}, u32[]{:S(2)}, u32[]{:S(2)}) collective-permute-start(f32[7,2,64,2]{3,2,1,0:T(8,128)S(1)} %get-tuple-element.35), channel_id=1, source_target_pairs={{0,1},{1,2},{2,3},{4,5},{5,6},{6,7},{8,9},{9,10},{10,11},{12,13},{... | collective-permute-start | bytes 21512 | tf_op jit(solution)/shard_map/ppermute | solution.py:30
  27.8 5.0 %collective-permute-start.8 = (f32[14,192]{1,0:T(8,128)S(1)}, f32[14,192]{1,0:T(8,128)S(1)}, u32[]{:S(2)}, u32[]{:S(2)}) collective-permute-start(f32[14,192]{1,0:T(8,128)S(1)} %collective-permute-done.6), channel_id=1, source_target_pairs={{0,1},{1,2},{2,3},{3,4},{4,5},{5,6},{6,7},{7,8},{8,9},{9,10},{10,1... | collective-permute-start | bytes 32264 | tf_op jit(solution)/shard_map/ppermute | solution.py:129
  29.1 29.6 %collective-permute-start.16 = (f32[7,2,2,128]{3,2,1,0:T(2,128)S(1)}, f32[7,2,2,128]{3,2,1,0:T(2,128)S(1)}, u32[]{:S(2)}, u32[]{:S(2)}) collective-permute-start(f32[7,2,2,128]{3,2,1,0:T(2,128)S(1)} %get-tuple-element.38), channel_id=1, source_target_pairs={{4,0},{8,4},{12,8},{5,1},{9,5},{13,9},{6,2},{10,6},{14,10},{7,3},{... | collective-permute-start | bytes 43016 | tf_op jit(solution)/shard_map/ppermute | solution.py:30
  32.8 5.0 %collective-permute-start.10 = (f32[14,192]{1,0:T(8,128)S(1)}, f32[14,192]{1,0:T(8,128)S(1)}, u32[]{:S(2)}, u32[]{:S(2)}) collective-permute-start(f32[14,192]{1,0:T(8,128)S(1)} %collective-permute-done.8), channel_id=1, source_target_pairs={{0,1},{1,2},{2,3},{3,4},{4,5},{5,6},{6,7},{7,8},{8,9},{9,10},{10,1... | collective-permute-start | bytes 32264 | tf_op jit(solution)/shard_map/ppermute | solution.py:129
  37.8 5.9 %collective-permute-start.12 = (f32[14,192]{1,0:T(8,128)S(1)}, f32[14,192]{1,0:T(8,128)S(1)}, u32[]{:S(2)}, u32[]{:S(2)}) collective-permute-start(f32[14,192]{1,0:T(8,128)S(1)} %collective-permute-done.10), channel_id=1, source_target_pairs={{0,1},{1,2},{2,3},{3,4},{4,5},{5,6},{6,7},{7,8},{8,9},{9,10},{10,1... | collective-permute-start | bytes 32264 | tf_op jit(solution)/shard_map/ppermute | solution.py:129
  38.7 10.8 %collective-permute-start.13 = (f32[14,192]{1,0:T(8,128)S(1)}, f32[14,192]{1,0:T(8,128)S(1)}, u32[]{:S(2)}, u32[]{:S(2)}) collective-permute-start(f32[14,192]{1,0:T(8,128)S(1)} %collective-permute-done.11), channel_id=1, source_target_pairs={{0,15},{1,0},{2,1},{3,2},{4,3},{5,4},{6,5},{7,6},{8,7},{9,8},{10,9... | collective-permute-start | bytes 32264 | tf_op jit(solution)/shard_map/ppermute | solution.py:136
  43.7 7.6 %collective-permute-start.14 = (f32[14,192]{1,0:T(8,128)S(1)}, f32[14,192]{1,0:T(8,128)S(1)}, u32[]{:S(2)}, u32[]{:S(2)}) collective-permute-start(f32[14,192]{1,0:T(8,128)S(1)} %collective-permute-done.12), channel_id=1, source_target_pairs={{0,1},{1,2},{2,3},{3,4},{4,5},{5,6},{6,7},{7,8},{8,9},{9,10},{10,1... | collective-permute-start | bytes 32264 | tf_op jit(solution)/shard_map/ppermute | solution.py:129
  49.4 9.2 %collective-permute-start.17 = (f32[7,2,2,128]{3,2,1,0:T(2,128)S(1)}, f32[7,2,2,128]{3,2,1,0:T(2,128)S(1)}, u32[]{:S(2)}, u32[]{:S(2)}) collective-permute-start(f32[7,2,2,128]{3,2,1,0:T(2,128)S(1)} %get-tuple-element.37), channel_id=1, source_target_pairs={{0,4},{4,8},{8,12},{1,5},{5,9},{9,13},{2,6},{6,10},{10,14},{3,7},{... | collective-permute-start | bytes 43016 | tf_op jit(solution)/shard_map/ppermute | solution.py:30
  61.7 6.0 %collective-permute-start.20 = (f32[14,192]{1,0:T(8,128)S(1)}, f32[14,192]{1,0:T(8,128)S(1)}, u32[]{:S(2)}, u32[]{:S(2)}) collective-permute-start(f32[14,192]{1,0:T(8,128)S(1)} %reshape.359), channel_id=1, source_target_pairs={{0,1},{1,2},{2,3},{3,4},{4,5},{5,6},{6,7},{7,8},{8,9},{9,10},{10,1... | collective-permute-start | bytes 32264 | tf_op jit(solution)/shard_map/ppermute | solution.py:129
  61.7 6.2 %collective-permute-start.21 = (f32[14,192]{1,0:T(8,128)S(1)}, f32[14,192]{1,0:T(8,128)S(1)}, u32[]{:S(2)}, u32[]{:S(2)}) collective-permute-start(f32[14,192]{1,0:T(8,128)S(1)} %reshape.359), channel_id=1, source_target_pairs={{0,15},{1,0},{2,1},{3,2},{4,3},{5,4},{6,5},{7,6},{8,7},{9,8},{10,9... | collective-permute-start | bytes 32264 | tf_op jit(solution)/shard_map/ppermute | solution.py:136
  67.7 5.9 %collective-permute-start.22 = (f32[14,192]{1,0:T(8,128)S(1)}, f32[14,192]{1,0:T(8,128)S(1)}, u32[]{:S(2)}, u32[]{:S(2)}) collective-permute-start(f32[14,192]{1,0:T(8,128)S(1)} %collective-permute-done.20), channel_id=1, source_target_pairs={{0,1},{1,2},{2,3},{3,4},{4,5},{5,6},{6,7},{7,8},{8,9},{9,10},{10,1... | collective-permute-start | bytes 32264 | tf_op jit(solution)/shard_map/ppermute | solution.py:129
  67.9 5.8 %collective-permute-start.23 = (f32[14,192]{1,0:T(8,128)S(1)}, f32[14,192]{1,0:T(8,128)S(1)}, u32[]{:S(2)}, u32[]{:S(2)}) collective-permute-start(f32[14,192]{1,0:T(8,128)S(1)} %collective-permute-done.21), channel_id=1, source_target_pairs={{0,15},{1,0},{2,1},{3,2},{4,3},{5,4},{6,5},{7,6},{8,7},{9,8},{10,9... | collective-permute-start | bytes 32264 | tf_op jit(solution)/shard_map/ppermute | solution.py:136
  73.5 5.9 %collective-permute-start.24 = (f32[14,192]{1,0:T(8,128)S(1)}, f32[14,192]{1,0:T(8,128)S(1)}, u32[]{:S(2)}, u32[]{:S(2)}) collective-permute-start(f32[14,192]{1,0:T(8,128)S(1)} %collective-permute-done.22), channel_id=1, source_target_pairs={{0,1},{1,2},{2,3},{3,4},{4,5},{5,6},{6,7},{7,8},{8,9},{9,10},{10,1... | collective-permute-start | bytes 32264 | tf_op jit(solution)/shard_map/ppermute | solution.py:129
  73.7 5.9 %collective-permute-start.25 = (f32[14,192]{1,0:T(8,128)S(1)}, f32[14,192]{1,0:T(8,128)S(1)}, u32[]{:S(2)}, u32[]{:S(2)}) collective-permute-start(f32[14,192]{1,0:T(8,128)S(1)} %collective-permute-done.23), channel_id=1, source_target_pairs={{0,15},{1,0},{2,1},{3,2},{4,3},{5,4},{6,5},{7,6},{8,7},{9,8},{10,9... | collective-permute-start | bytes 32264 | tf_op jit(solution)/shard_map/ppermute | solution.py:136
  79.4 5.9 %collective-permute-start.26 = (f32[14,192]{1,0:T(8,128)S(1)}, f32[14,192]{1,0:T(8,128)S(1)}, u32[]{:S(2)}, u32[]{:S(2)}) collective-permute-start(f32[14,192]{1,0:T(8,128)S(1)} %collective-permute-done.24), channel_id=1, source_target_pairs={{0,1},{1,2},{2,3},{3,4},{4,5},{5,6},{6,7},{7,8},{8,9},{9,10},{10,1... | collective-permute-start | bytes 32264 | tf_op jit(solution)/shard_map/ppermute | solution.py:129
  79.6 5.9 %collective-permute-start.27 = (f32[14,192]{1,0:T(8,128)S(1)}, f32[14,192]{1,0:T(8,128)S(1)}, u32[]{:S(2)}, u32[]{:S(2)}) collective-permute-start(f32[14,192]{1,0:T(8,128)S(1)} %collective-permute-done.25), channel_id=1, source_target_pairs={{0,15},{1,0},{2,1},{3,2},{4,3},{5,4},{6,5},{7,6},{8,7},{9,8},{10,9... | collective-permute-start | bytes 32264 | tf_op jit(solution)/shard_map/ppermute | solution.py:136
  85.3 5.9 %collective-permute-start.28 = (f32[14,192]{1,0:T(8,128)S(1)}, f32[14,192]{1,0:T(8,128)S(1)}, u32[]{:S(2)}, u32[]{:S(2)}) collective-permute-start(f32[14,192]{1,0:T(8,128)S(1)} %collective-permute-done.26), channel_id=1, source_target_pairs={{0,1},{1,2},{2,3},{3,4},{4,5},{5,6},{6,7},{7,8},{8,9},{9,10},{10,1... | collective-permute-start | bytes 32264 | tf_op jit(solution)/shard_map/ppermute | solution.py:129
  85.4 5.9 %collective-permute-start.29 = (f32[14,192]{1,0:T(8,128)S(1)}, f32[14,192]{1,0:T(8,128)S(1)}, u32[]{:S(2)}, u32[]{:S(2)}) collective-permute-start(f32[14,192]{1,0:T(8,128)S(1)} %collective-permute-done.27), channel_id=1, source_target_pairs={{0,15},{1,0},{2,1},{3,2},{4,3},{5,4},{6,5},{7,6},{8,7},{9,8},{10,9... | collective-permute-start | bytes 32264 | tf_op jit(solution)/shard_map/ppermute | solution.py:136
  91.1 5.9 %collective-permute-start.30 = (f32[14,192]{1,0:T(8,128)S(1)}, f32[14,192]{1,0:T(8,128)S(1)}, u32[]{:S(2)}, u32[]{:S(2)}) collective-permute-start(f32[14,192]{1,0:T(8,128)S(1)} %collective-permute-done.28), channel_id=1, source_target_pairs={{0,1},{1,2},{2,3},{3,4},{4,5},{5,6},{6,7},{7,8},{8,9},{9,10},{10,1... | collective-permute-start | bytes 32264 | tf_op jit(solution)/shard_map/ppermute | solution.py:129
  91.3 5.9 %collective-permute-start.31 = (f32[14,192]{1,0:T(8,128)S(1)}, f32[14,192]{1,0:T(8,128)S(1)}, u32[]{:S(2)}, u32[]{:S(2)}) collective-permute-start(f32[14,192]{1,0:T(8,128)S(1)} %collective-permute-done.29), channel_id=1, source_target_pairs={{0,15},{1,0},{2,1},{3,2},{4,3},{5,4},{6,5},{7,6},{8,7},{9,8},{10,9... | collective-permute-start | bytes 32264 | tf_op jit(solution)/shard_map/ppermute | solution.py:136
  97.0 5.9 %collective-permute-start.32 = (f32[14,192]{1,0:T(8,128)S(1)}, f32[14,192]{1,0:T(8,128)S(1)}, u32[]{:S(2)}, u32[]{:S(2)}) collective-permute-start(f32[14,192]{1,0:T(8,128)S(1)} %collective-permute-done.30), channel_id=1, source_target_pairs={{0,1},{1,2},{2,3},{3,4},{4,5},{5,6},{6,7},{7,8},{8,9},{9,10},{10,1... | collective-permute-start | bytes 32264 | tf_op jit(solution)/shard_map/ppermute | solution.py:129
  97.2 21.6 %collective-permute-start.33 = (f32[14,192]{1,0:T(8,128)S(1)}, f32[14,192]{1,0:T(8,128)S(1)}, u32[]{:S(2)}, u32[]{:S(2)}) collective-permute-start(f32[14,192]{1,0:T(8,128)S(1)} %collective-permute-done.31), channel_id=1, source_target_pairs={{0,15},{1,0},{2,1},{3,2},{4,3},{5,4},{6,5},{7,6},{8,7},{9,8},{10,9... | collective-permute-start | bytes 32264 | tf_op jit(solution)/shard_map/ppermute | solution.py:136
  102.8 20.7 %collective-permute-start.34 = (f32[14,192]{1,0:T(8,128)S(1)}, f32[14,192]{1,0:T(8,128)S(1)}, u32[]{:S(2)}, u32[]{:S(2)}) collective-permute-start(f32[14,192]{1,0:T(8,128)S(1)} %collective-permute-done.32), channel_id=1, source_target_pairs={{0,1},{1,2},{2,3},{3,4},{4,5},{5,6},{6,7},{7,8},{8,9},{9,10},{10,1... | collective-permute-start | bytes 32264 | tf_op jit(solution)/shard_map/ppermute | solution.py:129
  103.3 27.4 %collective-permute-start.38 = (f32[7,2,64,2]{3,2,1,0:T(8,128)S(1)}, f32[7,2,64,2]{3,2,1,0:T(8,128)S(1)}, u32[]{:S(2)}, u32[]{:S(2)}) collective-permute-start(f32[7,2,64,2]{3,2,1,0:T(8,128)S(1)} %get-tuple-element.24), channel_id=1, source_target_pairs={{1,0},{2,1},{3,2},{5,4},{6,5},{7,6},{9,8},{10,9},{11,10},{13,12},{... | collective-permute-start | bytes 21512 | tf_op jit(solution)/shard_map/ppermute | solution.py:30
  110.3 20.4 %collective-permute-start.39 = (f32[7,2,64,2]{3,2,1,0:T(8,128)S(1)}, f32[7,2,64,2]{3,2,1,0:T(8,128)}, u32[]{:S(2)}, u32[]{:S(2)}) collective-permute-start(f32[7,2,64,2]{3,2,1,0:T(8,128)S(1)} %get-tuple-element.23), channel_id=1, source_target_pairs={{0,1},{1,2},{2,3},{4,5},{5,6},{6,7},{8,9},{9,10},{10,11},{12,13},{... | collective-permute-start | bytes 21512 | tf_op jit(solution)/shard_map/ppermute | solution.py:30
  112.3 19.7 %collective-permute-start.36 = (f32[7,2,2,128]{3,2,1,0:T(2,128)S(1)}, f32[7,2,2,128]{3,2,1,0:T(2,128)}, u32[]{:S(2)}, u32[]{:S(2)}) collective-permute-start(f32[7,2,2,128]{3,2,1,0:T(2,128)S(1)} %get-tuple-element.26), channel_id=1, source_target_pairs={{4,0},{8,4},{12,8},{5,1},{9,5},{13,9},{6,2},{10,6},{14,10},{7,3},{... | collective-permute-start | bytes 43016 | tf_op jit(solution)/shard_map/ppermute | solution.py:30
  118.8 13.2 %collective-permute-start.37 = (f32[7,2,2,128]{3,2,1,0:T(2,128)S(1)}, f32[7,2,2,128]{3,2,1,0:T(2,128)}, u32[]{:S(2)}, u32[]{:S(2)}) collective-permute-start(f32[7,2,2,128]{3,2,1,0:T(2,128)S(1)} %get-tuple-element.25), channel_id=1, source_target_pairs={{0,4},{4,8},{8,12},{1,5},{5,9},{9,13},{2,6},{6,10},{10,14},{3,7},{... | collective-permute-start | bytes 43016 | tf_op jit(solution)/shard_map/ppermute | solution.py:30
  124.0 4.9 %collective-permute-start.35 = (f32[14,3072]{1,0:T(8,128)S(1)}, f32[14,3072]{1,0:T(8,128)S(1)}, u32[]{:S(2)}, u32[]{:S(2)}) collective-permute-start(f32[14,3072]{1,0:T(8,128)S(1)} %dynamic_update_slice.127), channel_id=1, source_target_pairs={{0,16},{16,0},{1,17},{17,1},{2,18},{18,2},{3,19},{19,3},{4,20},{20... | collective-permute-start | bytes 516104 | tf_op jit(solution)/shard_map/ppermute | solution.py:21
  (11 other events, 73.1 us)
